TPU v7x, 128 devices: a whole 4x4x4 slice. The times are simulated.
128 devices in a mesh: sec: 2 (over core), tile: 64 (over y, x, z).
Axes of the slice: x: 4, y: 4, z: 4, core: 2. Of those that a mesh axis runs over, the one named last changes fastest.
Arguments:
- land_wind: float32 [16384, 128], P(('sec', 'tile')), may hold values from 0.15 to 0.9
- land_moist: float32 [16384, 128], P(('sec', 'tile')), may hold values from 0 to 0.3
- texture: int32 [16384, 128], P(('sec', 'tile')), may hold values from 0 to 3
- land_index: int32 [16384, 128], P(('sec', 'tile')), may hold values from 0 to 32767
- erod_map: float32 [4194304], P(('sec', 'tile')), may hold values from 0.2 to 1
- mass_frac: float32 [4, 12], replicated, may hold values from 0.02 to 0.3
- blast_table: float32 [4, 8, 12], replicated, may hold values from 0.05 to 1
- dest_tile: int32 [16384, 1], P(('sec', 'tile')), may hold values from 0 to 127; in each aligned block of 128 rows (0 to 127, 128 to 255, ...) at most 2 rows name the same one
- regrid_w: bfloat16 [16384, 128, 256], P(('sec', 'tile')), may hold values from 0 to 0.25, as said below
- atm_state: float32 [3, 16, 32768], P(None, None, ('sec', 'tile')), may hold values from -5 to 5
- dust_mix: float32 [8, 16, 32768], P(None, None, ('sec', 'tile')), may hold values from 0 to 1
- mixing: float32 [15, 32768], P(None, ('sec', 'tile')), may hold values from 0.1 to 10
- settle: float32 [8], replicated, may hold values from 0.05 to 0.5
Outputs:
- land_fields: float32 [2, 16384, 128], P(None, ('sec', 'tile'))
- dust_out: float32 [8, 16, 32768], P(None, None, ('sec', 'tile'))
Inputs may be any that keep to these rules, and one draw needn't show every extreme that they name: `land_index`: each land cell's index points into its own device's 32768 cells of erod_map. `dest_tile`: among the 128 blocks of one device at most 2 name the same tile, a bound that some block reaches. `regrid_w`: each land cell has 1 to 4 positive weights, of 0.05 or more, on adjacent columns of its tile, and 0 elsewhere.
All inputs are finite; a program needn't handle non-finite values.
Results may differ from a plain program's by a relative error of at most 0.0023.
Values may be sent and summed in bfloat16 or wider, within the bound.
No kernel may reach another device: no remote copies, remote signals or barrier semaphores. Data moves between devices by JAX's collectives and lax.ppermute only.
A program may use at most 64 MiB of HBM per device.

v0:
```python
import jax
import jax.numpy as jnp
from jax import lax
from jax.sharding import PartitionSpec as P


def threshold_table(count):
    diameter = 4e-05 * jnp.power(jnp.float32(1.35), jnp.arange(count).astype(jnp.float32))
    return jnp.sqrt(0.0123 * (2160.0 * 9.81 * diameter + 0.0003 / (1.227 * diameter)))


def emit(wind_rows, moist_rows, texture_rows, erodible, mass_frac, blast_table, base_thresh):
    high = lax.Precision.HIGHEST
    thresh = base_thresh[:, None, None] * jnp.sqrt(1.0 + 12.1 * moist_rows)[None]
    classes = jnp.arange(mass_frac.shape[0])
    onehot = (texture_rows[None] == classes[:, None, None]).astype(jnp.float32)
    fraction = jnp.einsum("tb,tnl->bnl", mass_frac, onehot, precision=high)
    speed = wind_rows[None]
    salt = (
        40.0
        * fraction
        * erodible[None]
        * (speed + thresh)
        * jnp.maximum(speed * speed - thresh * thresh, 0.0)
    )
    blasted = jnp.einsum("tkb,bnl->tknl", blast_table, salt, precision=high)
    emission = jnp.sum(blasted * onehot[:, None], axis=0)
    return jnp.transpose(emission, (1, 0, 2)).astype(jnp.bfloat16)


def solve(right_side, coupling, sinking):
    levels = right_side.shape[1]
    sink_col = sinking[:, None]
    zero_row = jnp.zeros_like(coupling[0])
    ratios = []
    partial_value = []
    ratio_prev = None
    part_prev = None
    for level in range(levels):
        lower_c = coupling[level - 1] if level > 0 else zero_row
        upper_c = coupling[level] if level < levels - 1 else zero_row
        diagonal = 1.0 + lower_c[None] + upper_c[None] + sink_col
        if level == 0:
            pivot = diagonal
            part_now = right_side[:, level] / pivot
        else:
            pivot = diagonal + lower_c[None] * ratio_prev
            part_now = (right_side[:, level] + lower_c[None] * part_prev) / pivot
        if level < levels - 1:
            ratio_now = -(upper_c[None] + sink_col) / pivot
        else:
            ratio_now = jnp.zeros_like(pivot)
        ratios.append(ratio_now)
        partial_value.append(part_now)
        ratio_prev = ratio_now
        part_prev = part_now
    result = [None] * levels
    result[levels - 1] = partial_value[levels - 1]
    for level in range(levels - 2, -1, -1):
        result[level] = partial_value[level] - ratios[level] * result[level + 1]
    return jnp.stack(result, axis=1)


def on_device(
    land_wind,
    land_moist,
    texture,
    land_index,
    erod_map,
    mass_frac,
    blast_table,
    dest_tile,
    regrid_w,
    atm_state,
    dust_mix,
    mixing,
    settle,
):
    high = lax.Precision.HIGHEST
    nblocks, ncells = land_wind.shape
    columns = atm_state.shape[2]
    nbins = blast_table.shape[1]
    devices = lax.axis_size(("sec", "tile"))
    state = solve(atm_state, mixing, jnp.zeros((3,), jnp.float32))
    speed = jnp.sqrt(state[0, 0] ** 2 + state[1, 0] ** 2 + 0.25)
    surface = jnp.stack([speed, state[2, 0]]).astype(jnp.bfloat16).reshape(1, 2 * columns)
    gathered = lax.all_gather(surface, ("sec", "tile"), axis=0, tiled=True)
    base_thresh = threshold_table(mass_frac.shape[1])
    erodible = erod_map[land_index]
    emission = emit(land_wind, land_moist, texture, erodible, mass_frac, blast_table, base_thresh)
    partial_flux = jnp.einsum(
        "gkl,gla->gka", emission, regrid_w, preferred_element_type=jnp.float32
    )
    flat_flux = partial_flux.reshape(nblocks, nbins * columns)
    targets = dest_tile[:, 0]
    onehot = (targets[:, None] == jnp.arange(devices)[None, :]).astype(jnp.float32)
    capacity = max(2, 2 * nblocks // devices)
    before = jnp.cumsum(onehot, axis=0) - onehot
    ranking = jnp.sum(before * onehot, axis=1).astype(jnp.int32)
    slot_of = targets * capacity + ranking
    placing = (jnp.arange(devices * capacity)[:, None] == slot_of[None, :]).astype(jnp.float32)
    outgoing = jnp.dot(placing, flat_flux, precision=high).reshape(
        devices, capacity * nbins * columns
    )
    incoming = lax.all_to_all(
        outgoing.astype(jnp.bfloat16), ("sec", "tile"), split_axis=0, concat_axis=0, tiled=True
    ).astype(outgoing.dtype)
    flux = jnp.sum(incoming.reshape(devices * capacity, nbins, columns), axis=0)
    flux = flux * (float(columns) / float(ncells * nblocks))
    loaded = dust_mix.at[:, 0, :].add(flux)
    dust_out = solve(loaded, mixing, settle)
    picked = jnp.dot(onehot.astype(jnp.bfloat16), gathered, preferred_element_type=jnp.float32)
    picked = picked.astype(jnp.bfloat16).reshape(nblocks, 2, columns)
    numer = jnp.einsum("gla,gka->kgl", regrid_w, picked, preferred_element_type=jnp.float32)
    denom = jnp.sum(regrid_w, axis=2, dtype=jnp.float32)
    land_fields = jnp.stack([numer[0] / denom, 0.5 * land_moist + 0.5 * numer[1] / denom])
    return (land_fields, dust_out)


def solution(mesh):
    in_specs = (
        P(("sec", "tile"), None),
        P(("sec", "tile"), None),
        P(("sec", "tile"), None),
        P(("sec", "tile"), None),
        P(("sec", "tile")),
        P(),
        P(),
        P(("sec", "tile"), None),
        P(("sec", "tile"), None, None),
        P(None, None, ("sec", "tile")),
        P(None, None, ("sec", "tile")),
        P(None, ("sec", "tile")),
        P(),
    )
    out_specs = (P(None, ("sec", "tile"), None), P(None, None, ("sec", "tile")))
    return jax.shard_map(
        on_device, mesh=mesh, in_specs=in_specs, out_specs=out_specs, check_vma=False
    )
```

profile of v0, /device:TPU:1, one launch (start us, length us, event | category | flops | bytes accessed | tf_op | source)
XLA Modules:
  0.0 481.6 jit_solution(7172732893140782613)
XLA Ops:
  0.6 1.0 fusion.78
  1.7 1.0 broadcast_add_fusion.1
  2.7 0.9 fusion.79
  3.6 1.2 fusion.77
  5.4 321.0 %all-gather = bf16[128,1,512]{2,1,0:T(2,128)(2,1)S(1)} all-gather(bf16[1,1,512]{2,1,0:T(2,128)(2,1)S(1)} %reshape.27177), channel_id=1, replica_groups=mesh['sec'=2,'tile'=64] {'sec','tile'}, dimensions={0}, use_global_device_ids=true | all-gather | bytes 132096 | tf_op jit(solution)/shard_map/all_gather | solution.py:87
  326.4 0.7 fusion.17
  327.1 0.9 convolution_convert_fusion.1
  328.1 5.8 %convert_reduce_fusion = f32[128,128]{1,0:T(8,128)S(1)} fusion(bf16[128,128,256]{2,1,0:T(8,128)(2,1)} %param.23), kind=kLoop, calls=%fused_computation.1 | loop fusion | flops 8372224 | bytes 8454144 | tf_op jit(solution)/shard_map/reduce_sum | solution.py:115
  333.9 2.3 convolution_bitcast_fusion
  336.3 90.5 %gather_fusion = f32[16384]{0:T(1024)S(1)} fusion(f32[32768]{0:T(1024)S(1)} %copy-done, s32[16384]{0:T(1024)S(1)} %fusion.15), kind=kCustom, calls=%fused_computation | custom fusion | bytes 196608 | tf_op jit(solution)/shard_map/gather | solution.py:89
  427.1 0.8 fusion.4
  427.9 1.9 fusion
  429.8 4.6 fusion.7
  435.2 1.0 convolution_convert_fusion
  436.2 1.9 convert_element_type.86
  438.7 7.0 %reduce.4 = bf16[128,4096]{1,0:T(8,128)(2,1)S(1)} reduce(bf16[128,1,4096]{2,1,0:T(2,128)(2,1)S(1)} %convert_element_type.86, bf16[]{:T(256)} %broadcast.18933), dimensions={1}, to_apply=%convert_element_type.86.reduce_sub_computation | reduce | bytes 2097154 | tf_op jit(solution)/shard_map/convert_element_type | solution.py:106
  445.7 1.6 reshape.27184
  447.3 3.8 all-to-all-start
  451.1 0.7 pad_maximum_fusion
  451.9 16.8 %all-to-all-done = bf16[128,2,2048]{2,1,0:T(2,128)(2,1)S(1)} async-done(((bf16[128,2,2048]{2,1,0:T(2,128)(2,1)}), bf16[128,2,2048]{2,1,0:T(2,128)(2,1)S(1)}, u32[]{:S(2)}, u32[]{:S(2)}) %all-to-all-start) | async-done | bytes 1048608 | tf_op jit(solution)/shard_map/all_to_all | solution.py:105
  468.7 1.0 reshape.27185
  469.7 7.5 %convert_reduce_fusion.1 = f32[128,4096]{1,0:T(8,128)} fusion(bf16[128,1,4096]{2,1,0:T(2,128)(2,1)S(1)} %reshape.27185), kind=kLoop, calls=%fused_computation.5 | loop fusion | flops 524288 | bytes 3145728 | tf_op jit(solution)/shard_map/convert_element_type | solution.py:107
  477.2 1.7 reshape.27164
  480.9 0.7 copy.100
  (105 shorter events, 4.0 us)
Async XLA Ops:
  0.6 335.6 %copy-start = (f32[32768]{0:T(1024)S(1)}, f32[32768]{0:T(1024)}, u32[]{:S(2)}) copy-start(f32[32768]{0:T(1024)} %param.19) | copy-start | bytes 393220
  1.6 3.4 copy-start.14
  1.6 3.4 copy-start.16
  1.6 3.4 copy-start.18
  1.7 3.5 copy-start.24
  2.7 2.2 copy-start.8
  2.7 2.4 copy-start.10
  2.7 2.4 copy-start.12
  2.7 2.4 copy-start.20
  2.7 2.4 copy-start.22
  2.7 2.5 copy-start.27
  2.7 2.6 copy-start.29
  328.0 5.8 %copy-start.1 = (bf16[128,128,256]{2,1,0:T(8,128)(2,1)S(1)}, bf16[128,128,256]{2,1,0:T(8,128)(2,1)}, u32[]{:S(2)}) copy-start(bf16[128,128,256]{2,1,0:T(8,128)(2,1)} %param.23) | copy-start | bytes 25165828
  333.8 2.4 copy-start.6
  336.3 90.6 %copy-start.2 = (f32[128,128]{1,0:T(8,128)S(1)}, f32[128,128]{1,0:T(8,128)}, u32[]{:S(2)}) copy-start(f32[128,128]{1,0:T(8,128)} %param.15) | copy-start | bytes 196612
  336.3 90.6 %copy-start.5 = (s32[128,128]{1,0:T(8,128)S(1)}, s32[128,128]{1,0:T(8,128)}, u32[]{:S(2)}) copy-start(s32[128,128]{1,0:T(8,128)} %param.17) | copy-start | bytes 196612
  336.3 90.7 %copy-start.4 = (f32[128,128]{1,0:T(8,128)S(1)}, f32[128,128]{1,0:T(8,128)}, u32[]{:S(2)}) copy-start(f32[128,128]{1,0:T(8,128)} %param.16) | copy-start | bytes 196612
  336.3 90.7 %copy-start.32 = (f32[4,12]{1,0:T(4,128)S(1)}, f32[4,12]{1,0:T(4,128)}, u32[]{:S(2)}) copy-start(f32[4,12]{1,0:T(4,128)} %param.20) | copy-start | bytes 580
  426.9 1.0 copy-start.26
  445.7 6.1 %copy-start.3 = (f32[8,16,256]{2,1,0:T(8,128)S(1)}, f32[8,16,256]{2,1,0:T(8,128)}, u32[]{:S(2)}) copy-start(f32[8,16,256]{2,1,0:T(8,128)} %param.25) | copy-start | bytes 393220
  447.3 21.3 %all-to-all-start = ((bf16[128,2,2048]{2,1,0:T(2,128)(2,1)}), bf16[128,2,2048]{2,1,0:T(2,128)(2,1)S(1)}, u32[]{:S(2)}, u32[]{:S(2)}) async-start(bf16[128,2,2048]{2,1,0:T(2,128)(2,1)} %reshape.27184), calls=%async_computation | async-start | bytes 2097152 | tf_op jit(solution)/shard_map/all_to_all | solution.py:105
  479.0 0.8 copy-start.15
  479.0 0.8 copy-start.17
  479.0 0.8 copy-start.19
  (10 other events, 6.7 us)
where the time goes:
time: 482 us
  blocking collectives  321 us (67%)
  local copies, waits for them, and re-layouts  101 us (21%)
  other arithmetic  26 us (5%)
  waiting for transfers between devices  16.8 us (3%)
  matrix products  11.4 us (2%)
    all_gather x1, blocking collectives, on_device(): gathered = lax.all_gather(surface, ('sec', 'tile'), axis=0, tiled=True)  321 us
    gather x1, local copies, waits for them, and re-layouts, on_device(): erodible = erod_map[land_index]  90.5 us
    all_to_all x1, waiting for transfers between devices, on_device(): lax.all_to_all(outgoing.astype(jnp.bfloat16), ('sec', 'tile'), split_axis...  16.8 us
  transfers between devices with their start and end apart: 1, of which 1 were waited for; matrix products, arithmetic and copies ran while one was open for 0% of the time, Pallas kernels for 0%

commit v1 on v0

--- a/solution.py
+++ b/solution.py
@@ -84,7 +84,12 @@
     state = solve(atm_state, mixing, jnp.zeros((3,), jnp.float32))
     speed = jnp.sqrt(state[0, 0] ** 2 + state[1, 0] ** 2 + 0.25)
     surface = jnp.stack([speed, state[2, 0]]).astype(jnp.bfloat16).reshape(1, 2 * columns)
-    gathered = lax.all_gather(surface, ("sec", "tile"), axis=0, tiled=True)
+    gathered = jnp.concatenate(
+        lax.all_to_all(
+            jnp.stack([surface] * lax.axis_size(("sec", "tile"))), ("sec", "tile"), 0, 0
+        ),
+        axis=0,
+    )
     base_thresh = threshold_table(mass_frac.shape[1])
     erodible = erod_map[land_index]
     emission = emit(land_wind, land_moist, texture, erodible, mass_frac, blast_table, base_thresh)

time: 482 us -> 184 us (0.38)
  blocking collectives: 321 us -> 0 us
  starting transfers between devices: 3.78 us -> 21.3 us
    all_gather x1 -> x0, blocking collectives: 321 us -> none  [on_device(): gathered = lax.all_gather(surface, ('sec', 'tile'), axis=0, tiled=True)]
    all_to_all x0 -> x1, starting transfers between devices: none -> 11.5 us  [on_device(): lax.all_to_all(jnp.stack([surface] * lax.axis_size(('sec', 'tile'))), ('s...]
    all_to_all x1, starting transfers between devices: 3.78 us -> 9.77 us  [on_device(): lax.all_to_all(outgoing.astype(jnp.bfloat16), ('sec', 'tile'), split_axis...]
  transfers between devices with their start and end apart: 1 -> 2, of which waited for: 1 -> 1; matrix products, arithmetic and copies ran while one was open for 0% -> 54% of each run, Pallas kernels for 0% -> 0%
where the time goes in v1:
time: 184 us; the launch traced here: 183 us
  local copies, waits for them, and re-layouts  103 us (56%)
  other arithmetic  26.6 us (14%)
  starting transfers between devices  21.3 us (12%)
  waiting for transfers between devices  16.3 us (9%)
  matrix products  14.1 us (8%)
  between operations  2.04 us (1%)
    gather x1, local copies, waits for them, and re-layouts, on_device(): erodible = erod_map[land_index]  90.5 us
    all_to_all x1, waiting for transfers between devices, on_device(): lax.all_to_all(outgoing.astype(jnp.bfloat16), ('sec', 'tile'), split_axis...  16.2 us
    all_to_all x1, starting transfers between devices, on_device(): lax.all_to_all(jnp.stack([surface] * lax.axis_size(('sec', 'tile'))), ('s...  11.5 us
    all_to_all x1, starting transfers between devices, on_device(): lax.all_to_all(outgoing.astype(jnp.bfloat16), ('sec', 'tile'), split_axis...  9.77 us
    convert_element_type x1, other arithmetic, on_device(): incoming = lax.all_to_all(outgoing.astype(jnp.bfloat16), ('sec', 'tile'),...  7.46 us
    convert_element_type x1, other arithmetic, on_device(): outgoing.astype(jnp.bfloat16)  7.03 us
    dot_general x1, matrix products, on_device(): jnp.einsum('gla,gka->kgl', regrid_w, picked, preferred_element_type=jnp.f...  5.66 us
    reduce_sum x1, other arithmetic, on_device(): denom = jnp.sum(regrid_w, axis=2, dtype=jnp.float32)  5.65 us
  transfers between devices with their start and end apart: 2, of which 1 were waited for; matrix products, arithmetic and copies ran while one was open for 54% of the time, Pallas kernels for 0%

profile of v1, /device:TPU:1, one launch (start us, length us, event | category | flops | bytes accessed | tf_op | source)
XLA Modules:
  0.0 183.0 jit_solution(8447883691844025357)
XLA Ops:
  0.6 1.0 fusion.78
  1.7 1.0 broadcast_add_fusion.1
  2.9 0.9 fusion.79
  3.8 1.2 fusion.77
  6.3 1.4 reduce.4
  7.7 0.7 reshape.27182
  8.4 11.5 %all-to-all-start = ((bf16[128,2,256]{2,1,0:T(2,128)(2,1)}), bf16[128,2,256]{2,1,0:T(2,128)(2,1)S(1)}, u32[]{:S(2)}, u32[]{:S(2)}) async-start(bf16[128,2,256]{2,1,0:T(2,128)(2,1)} %reshape.27182), calls=%async_computation | async-start | bytes 262144 | tf_op jit(solution)/shard_map/all_to_all | solution.py:88
  19.9 5.6 %convert_reduce_fusion = f32[128,128]{1,0:T(8,128)S(1)} fusion(bf16[128,128,256]{2,1,0:T(8,128)(2,1)} %param.23), kind=kLoop, calls=%fused_computation.1 | loop fusion | flops 8372224 | bytes 8454144 | tf_op jit(solution)/shard_map/reduce_sum | solution.py:120
  25.7 90.5 %gather_fusion = f32[16384]{0:T(1024)S(1)} fusion(f32[32768]{0:T(1024)S(1)} %copy-done, s32[16384]{0:T(1024)S(1)} %fusion.15), kind=kCustom, calls=%fused_computation | custom fusion | bytes 196608 | tf_op jit(solution)/shard_map/gather | solution.py:94
  117.3 5.7 %convolution_bitcast_fusion = f32[2,128,128]{2,0,1:T(2,128)S(1)} fusion(bf16[128,2,256]{2,1,0:T(2,128)(2,1)S(1)} %reshape.27163, bf16[128,128,256]{2,1,0:T(8,128)(2,1)} %param.23), kind=kOutput, calls=%fused_computation.14 | convolution fusion | flops 16777216 | bytes 8650752 | tf_op jit(solution)/shard_map/gla,gka->kgl/dot_general | solution.py:119
  123.1 0.8 fusion.4
  124.0 1.8 fusion
  125.8 4.6 %fusion.7 = f32[128,8,256]{2,1,0:T(8,128)S(1)} fusion(bf16[128,128,256]{2,1,0:T(8,128)(2,1)} %param.23, bf16[8,128,128]{2,0,1:T(8,128)(2,1)S(1)} %fusion), kind=kOutput, calls=%fused_computation.17 | convolution fusion | flops 67108864 | bytes 9699328 | tf_op jit(solution)/shard_map/gkl,gla->gka/dot_general | solution.py:96
  130.7 1.0 convolution_convert_fusion
  131.7 1.9 %convert_element_type.84 = bf16[128,1,4096]{2,1,0:T(2,128)(2,1)S(1)} reshape(bf16[256,2048]{1,0:T(8,128)(2,1)S(1)} %convolution_convert_fusion) | data formatting | bytes 2097152 | tf_op jit(solution)/shard_map/convert_element_type | solution.py:111
  133.6 7.0 %reduce.5 = bf16[128,4096]{1,0:T(8,128)(2,1)S(1)} reduce(bf16[128,1,4096]{2,1,0:T(2,128)(2,1)S(1)} %convert_element_type.84, bf16[]{:T(256)} %broadcast.18935), dimensions={1}, to_apply=%convert_element_type.84.reduce_sub_computation | reduce | bytes 2097154 | tf_op jit(solution)/shard_map/convert_element_type | solution.py:111
  140.7 1.6 reshape.27184
  142.3 9.8 %all-to-all-start.1 = ((bf16[128,2,2048]{2,1,0:T(2,128)(2,1)}), bf16[128,2,2048]{2,1,0:T(2,128)(2,1)S(1)}, u32[]{:S(2)}, u32[]{:S(2)}) async-start(bf16[128,2,2048]{2,1,0:T(2,128)(2,1)} %reshape.27184), calls=%async_computation.1 | async-start | bytes 2097152 | tf_op jit(solution)/shard_map/all_to_all | solution.py:110
  152.1 0.7 fusion.75
  153.4 16.2 %all-to-all-done.1 = bf16[128,2,2048]{2,1,0:T(2,128)(2,1)S(1)} async-done(((bf16[128,2,2048]{2,1,0:T(2,128)(2,1)}), bf16[128,2,2048]{2,1,0:T(2,128)(2,1)S(1)}, u32[]{:S(2)}, u32[]{:S(2)}) %all-to-all-start.1) | async-done | bytes 1048608 | tf_op jit(solution)/shard_map/all_to_all | solution.py:110
  169.7 1.0 reshape.27185
  170.8 7.5 %convert_reduce_fusion.1 = f32[128,4096]{1,0:T(8,128)} fusion(bf16[128,1,4096]{2,1,0:T(2,128)(2,1)S(1)} %reshape.27185), kind=kLoop, calls=%fused_computation.5 | loop fusion | flops 524288 | bytes 3145728 | tf_op jit(solution)/shard_map/convert_element_type | solution.py:112
  178.2 1.7 reshape.27165
  182.3 0.7 copy.99
  (194 shorter events, 5.0 us)
Async XLA Ops:
  0.6 25.0 %copy-start = (f32[32768]{0:T(1024)S(1)}, f32[32768]{0:T(1024)}, u32[]{:S(2)}) copy-start(f32[32768]{0:T(1024)} %param.19) | copy-start | bytes 393220
  1.6 3.8 %copy-start.17 = (f32[1,256]{1,0:T(1,128)}, f32[1,256]{1,0:T(1,128)S(1)}, u32[]{:S(2)}) copy-start(f32[1,256]{1,0:T(1,128)S(1)} %get-tuple-element.116) | copy-start | bytes 3076
  1.6 3.8 %copy-start.19 = (f32[1,256]{1,0:T(1,128)}, f32[1,256]{1,0:T(1,128)S(1)}, u32[]{:S(2)}) copy-start(f32[1,256]{1,0:T(1,128)S(1)} %get-tuple-element.117) | copy-start | bytes 3076
  1.6 3.8 %copy-start.27 = (f32[1,256]{1,0:T(1,128)}, f32[1,256]{1,0:T(1,128)S(1)}, u32[]{:S(2)}) copy-start(f32[1,256]{1,0:T(1,128)S(1)} %get-tuple-element.110) | copy-start | bytes 3076
  1.7 3.8 %copy-start.38 = (f32[1,256]{1,0:T(1,128)}, f32[1,256]{1,0:T(1,128)S(1)}, u32[]{:S(2)}) copy-start(f32[1,256]{1,0:T(1,128)S(1)} %get-tuple-element.111) | copy-start | bytes 3076
  1.7 3.8 %copy-start.40 = (f32[1,256]{1,0:T(1,128)}, f32[1,256]{1,0:T(1,128)S(1)}, u32[]{:S(2)}) copy-start(f32[1,256]{1,0:T(1,128)S(1)} %get-tuple-element.112) | copy-start | bytes 3076
  1.7 3.8 %copy-start.42 = (f32[1,256]{1,0:T(1,128)}, f32[1,256]{1,0:T(1,128)S(1)}, u32[]{:S(2)}) copy-start(f32[1,256]{1,0:T(1,128)S(1)} %get-tuple-element.122) | copy-start | bytes 3076
  1.7 3.8 %copy-start.56 = (f32[1,256]{1,0:T(1,128)}, f32[1,256]{1,0:T(1,128)S(1)}, u32[]{:S(2)}) copy-start(f32[1,256]{1,0:T(1,128)S(1)} %get-tuple-element.113) | copy-start | bytes 3076
  1.7 3.8 %copy-start.58 = (f32[1,256]{1,0:T(1,128)}, f32[1,256]{1,0:T(1,128)S(1)}, u32[]{:S(2)}) copy-start(f32[1,256]{1,0:T(1,128)S(1)} %get-tuple-element.114) | copy-start | bytes 3076
  1.7 3.8 %copy-start.60 = (f32[1,256]{1,0:T(1,128)}, f32[1,256]{1,0:T(1,128)S(1)}, u32[]{:S(2)}) copy-start(f32[1,256]{1,0:T(1,128)S(1)} %get-tuple-element.115) | copy-start | bytes 3076
  1.7 3.8 %copy-start.66 = (f32[1,256]{1,0:T(1,128)}, f32[1,256]{1,0:T(1,128)S(1)}, u32[]{:S(2)}) copy-start(f32[1,256]{1,0:T(1,128)S(1)} %get-tuple-element.121) | copy-start | bytes 3076
  1.7 23.9 %copy-start.4 = (f32[1,256]{1,0:T(1,128)}, f32[1,256]{1,0:T(1,128)S(1)}, u32[]{:S(2)}) copy-start(f32[1,256]{1,0:T(1,128)S(1)} %get-tuple-element.119) | copy-start | bytes 3076
  1.7 23.9 %copy-start.10 = (f32[1,256]{1,0:T(1,128)}, f32[1,256]{1,0:T(1,128)S(1)}, u32[]{:S(2)}) copy-start(f32[1,256]{1,0:T(1,128)S(1)} %get-tuple-element.109) | copy-start | bytes 3076
  2.8 22.8 %copy-start.6 = (f32[1,256]{1,0:T(1,128)}, f32[1,256]{1,0:T(1,128)S(1)}, u32[]{:S(2)}) copy-start(f32[1,256]{1,0:T(1,128)S(1)} %get-tuple-element.108) | copy-start | bytes 3076
  3.8 21.8 %copy-start.8 = (f32[1,256]{1,0:T(1,128)}, f32[1,256]{1,0:T(1,128)S(1)}, u32[]{:S(2)}) copy-start(f32[1,256]{1,0:T(1,128)S(1)} %get-tuple-element.123) | copy-start | bytes 3076
  8.4 108.4 %all-to-all-start = ((bf16[128,2,256]{2,1,0:T(2,128)(2,1)}), bf16[128,2,256]{2,1,0:T(2,128)(2,1)S(1)}, u32[]{:S(2)}, u32[]{:S(2)}) async-start(bf16[128,2,256]{2,1,0:T(2,128)(2,1)} %reshape.27182), calls=%async_computation | async-start | bytes 262144 | tf_op jit(solution)/shard_map/all_to_all | solution.py:88
  19.9 5.7 %copy-start.16 = (s32[128,128]{1,0:T(8,128)S(1)}, s32[128,128]{1,0:T(8,128)}, u32[]{:S(2)}) copy-start(s32[128,128]{1,0:T(8,128)} %param.18) | copy-start | bytes 196612
  25.7 90.6 %copy-start.15 = (s32[128,128]{1,0:T(8,128)S(1)}, s32[128,128]{1,0:T(8,128)}, u32[]{:S(2)}) copy-start(s32[128,128]{1,0:T(8,128)} %param.17) | copy-start | bytes 196612
  25.7 90.7 %copy-start.73 = (s32[128,1]{0,1:T(1,128)S(1)}, s32[128,1]{0,1:T(1,128)}, u32[]{:S(2)}) copy-start(s32[128,1]{0,1:T(1,128)} %param.22) | copy-start | bytes 1540
  25.7 91.1 %copy-start.1 = (f32[128,128]{1,0:T(8,128)S(1)}, f32[128,128]{1,0:T(8,128)}, u32[]{:S(2)}) copy-start(f32[128,128]{1,0:T(8,128)} %param.15) | copy-start | bytes 196612
  117.2 5.8 %copy-start.14 = (f32[128,128]{1,0:T(8,128)S(1)}, f32[128,128]{1,0:T(8,128)}, u32[]{:S(2)}) copy-start(f32[128,128]{1,0:T(8,128)} %param.16) | copy-start | bytes 196612
  117.3 5.9 %copy-start.74 = (f32[4,12]{1,0:T(4,128)S(1)}, f32[4,12]{1,0:T(4,128)}, u32[]{:S(2)}) copy-start(f32[4,12]{1,0:T(4,128)} %param.20) | copy-start | bytes 580
  140.7 11.4 %copy-start.2 = (f32[8,16,256]{2,1,0:T(8,128)S(1)}, f32[8,16,256]{2,1,0:T(8,128)}, u32[]{:S(2)}) copy-start(f32[8,16,256]{2,1,0:T(8,128)} %param.25) | copy-start | bytes 393220
  142.3 27.4 %all-to-all-start.1 = ((bf16[128,2,2048]{2,1,0:T(2,128)(2,1)}), bf16[128,2,2048]{2,1,0:T(2,128)(2,1)S(1)}, u32[]{:S(2)}, u32[]{:S(2)}) async-start(bf16[128,2,2048]{2,1,0:T(2,128)(2,1)} %reshape.27184), calls=%async_computation.1 | async-start | bytes 2097152 | tf_op jit(solution)/shard_map/all_to_all | solution.py:110
  (53 other events, 64.3 us)
